TPU v7x, 32 devices: a whole 2x2x4 slice. The times are simulated.
32 devices in a mesh: section: 8 (over z, core), seq: 4 (over y, x).
Axes of the slice: x: 2, y: 2, z: 4, core: 2. Of those that a mesh axis runs over, the one named last changes fastest.
Arguments:
- queries: bfloat16 [8, 512, 8192], P('section', 'seq'), may hold values from -48 to 48
- key_states: bfloat16 [8, 512, 1024], P('section', 'seq'), may hold values from -6 to 6
- section_value_states: bfloat16 [8, 512, 1024], P('section', 'seq'), may hold values from -6 to 6
- out_grad: bfloat16 [8, 512, 8192], P('section', 'seq'), may hold values from -1.5 to 1.5
- layer_input: bfloat16 [8, 512, 8192], P('section', 'seq'), may hold values from -6 to 6
- doc_segments: int32 [8, 512], P('section', 'seq'), may hold values from 0 to 3, never falling along the last dimension, each value on 1 to 256 neighbouring positions
Outputs:
- query_grad: bfloat16 [8, 512, 8192], P('section', 'seq')
- key_grad: bfloat16 [8, 512, 1024], P('section', 'seq')
- weight_grad: bfloat16 [8, 8192, 1024], P('section', None, 'seq')
Inputs may be any that keep to these rules, and one draw needn't show every extreme that they name: `doc_segments`: document numbers never fall along a section's positions; a document holds at most 256 positions.
All inputs are finite; a program needn't handle non-finite values.
Results may differ from a plain program's by a relative error of at most 0.012.
The roundings to bfloat16 on the way count: a program that leaves them out, or rounds other values in their place, can miss the bound.
Values may be sent and summed in bfloat16 or wider, within the bound.
No kernel may reach another device: no remote copies, remote signals or barrier semaphores. Data moves between devices by JAX's collectives and lax.ppermute only.
A program may use at most 128 MiB of HBM per device.

v0:
```python
import math
import jax
import jax.numpy as jnp
from jax import lax
from jax.sharding import PartitionSpec as P

HEAD_WIDTH = 128


def group_pass(query_group, key_col, value_col, grad_group, allowed):
    scale_factor = 1.0 / math.sqrt(key_col.shape[1])

    def one_head(totals, head_inputs):
        query_one, grad_one = head_inputs
        key_acc, value_acc = totals
        scores = jnp.dot(query_one, key_col.T, preferred_element_type=jnp.float32) * scale_factor
        scores = jnp.where(allowed, scores, -jnp.inf)
        row_max = jnp.max(scores, axis=1, keepdims=True)
        weights = jnp.exp(scores - row_max)
        attention = weights / jnp.sum(weights, axis=1, keepdims=True)
        probs_low = attention.astype(jnp.bfloat16)
        attended = jnp.dot(probs_low, value_col, preferred_element_type=jnp.float32).astype(
            jnp.bfloat16
        )
        attended = lax.optimization_barrier(attended)
        row_delta = jnp.sum(
            grad_one.astype(jnp.float32) * attended.astype(jnp.float32), axis=1, keepdims=True
        )
        dprobs = jnp.dot(grad_one, value_col.T, preferred_element_type=jnp.float32)
        dscores = (attention * (dprobs - row_delta) * scale_factor).astype(jnp.bfloat16)
        query_part = jnp.dot(dscores, key_col, preferred_element_type=jnp.float32).astype(
            jnp.bfloat16
        )
        key_acc = key_acc + jnp.dot(dscores.T, query_one, preferred_element_type=jnp.float32)
        value_acc = value_acc + jnp.dot(probs_low.T, grad_one, preferred_element_type=jnp.float32)
        return ((key_acc, value_acc), query_part)

    starting = jnp.zeros(key_col.shape, jnp.float32)
    (key_acc, value_acc), query_parts = lax.scan(
        one_head, (starting, starting), (query_group, grad_group)
    )
    return (query_parts, key_acc.astype(jnp.bfloat16), value_acc.astype(jnp.bfloat16))


def attention_grads(query_cols, key_cols, value_cols, grad_cols, doc_ids):
    length = query_cols.shape[0]
    kv_heads = key_cols.shape[1] // HEAD_WIDTH
    q_heads = query_cols.shape[1] // HEAD_WIDTH
    group_size = q_heads // kv_heads
    position = jnp.arange(length, dtype=jnp.int32)
    allowed = (position[:, None] >= position[None, :]) & (doc_ids[:, None] == doc_ids[None, :])
    query_split = query_cols.reshape(length, kv_heads, group_size, HEAD_WIDTH).transpose(1, 2, 0, 3)
    grad_split = grad_cols.reshape(length, kv_heads, group_size, HEAD_WIDTH).transpose(1, 2, 0, 3)
    key_split = key_cols.reshape(length, kv_heads, HEAD_WIDTH).transpose(1, 0, 2)
    value_split = value_cols.reshape(length, kv_heads, HEAD_WIDTH).transpose(1, 0, 2)

    def per_group(inputs):
        return group_pass(inputs[0], inputs[1], inputs[2], inputs[3], allowed)

    query_parts, key_parts, value_parts = lax.map(
        per_group, (query_split, key_split, value_split, grad_split)
    )
    query_out = query_parts.transpose(2, 0, 1, 3).reshape(length, q_heads * HEAD_WIDTH)
    key_out = key_parts.transpose(1, 0, 2).reshape(length, kv_heads * HEAD_WIDTH)
    value_out = value_parts.transpose(1, 0, 2).reshape(length, kv_heads * HEAD_WIDTH)
    return (query_out, key_out, value_out)


def row_product(shard_rows, value_rows):
    return lax.dot_general(
        shard_rows, value_rows, (((0,), (0,)), ((), ())), preferred_element_type=jnp.float32
    )


def local(queries, key_states, section_value_states, out_grad, layer_input, doc_segments):
    section_count = lax.axis_size("section")
    mirror = [(i, section_count - 1 - i) for i in range(section_count)]
    mirror_rows = lax.ppermute(layer_input[0], "section", mirror)
    query_head, key_head, value_head, grad_head = (
        lax.all_to_all(queries[0], "seq", split_axis=1, concat_axis=0, tiled=True),
        lax.all_to_all(key_states[0], "seq", split_axis=1, concat_axis=0, tiled=True),
        lax.all_to_all(section_value_states[0], "seq", split_axis=1, concat_axis=0, tiled=True),
        lax.all_to_all(out_grad[0], "seq", split_axis=1, concat_axis=0, tiled=True),
    )
    doc_ids = lax.all_gather(doc_segments[0], "seq", axis=0, tiled=True)
    query_out, key_out, value_out = attention_grads(
        query_head, key_head, value_head, grad_head, doc_ids
    )
    query_back, key_back = (
        lax.all_to_all(query_out, "seq", split_axis=0, concat_axis=1, tiled=True),
        lax.all_to_all(key_out, "seq", split_axis=0, concat_axis=1, tiled=True),
    )
    both_rows = jnp.concatenate([layer_input[0], mirror_rows], axis=0)
    gathered = lax.all_gather(both_rows, "seq", axis=0, tiled=True)
    mirror_value = lax.ppermute(value_out, "section", mirror)
    seq_count = lax.axis_size("seq")
    chunk = value_out.shape[0] // seq_count
    both_values = jnp.stack(
        [value_out.reshape(seq_count, chunk, -1), mirror_value.reshape(seq_count, chunk, -1)],
        axis=1,
    ).reshape(2 * value_out.shape[0], value_out.shape[1])
    paired = row_product(gathered, both_values)
    return (query_back[None], key_back[None], paired.astype(jnp.bfloat16)[None])


def solution(mesh):
    in_specs = (
        P("section", "seq", None),
        P("section", "seq", None),
        P("section", "seq", None),
        P("section", "seq", None),
        P("section", "seq", None),
        P("section", "seq"),
    )
    out_specs = (P("section", "seq", None), P("section", "seq", None), P("section", None, "seq"))
    return jax.shard_map(local, mesh=mesh, in_specs=in_specs, out_specs=out_specs, check_vma=False)
```

profile of v0, /device:TPU:8, one launch (start us, length us, event | category | flops | bytes accessed | tf_op | source)
XLA Modules:
  0.0 332.5 jit_solution(17759359656926367715)
XLA Ops:
  9.0 3.7 %all-to-all-start.2 = ((bf16[128,4,256]{2,0,1:T(8,128)(2,1)}), bf16[128,4,256]{2,0,1:T(8,128)(2,1)S(1)}, u32[]{:S(2)}, u32[]{:S(2)}) async-start(bf16[128,4,256]{2,0,1:T(8,128)(2,1)} %copy.27), calls=%async_computation.2 | async-start | bytes 524288 | tf_op jit(solution)/shard_map/all_to_all | solution.py:81
  14.6 3.5 %all-to-all-done.2 = bf16[128,4,256]{2,0,1:T(8,128)(2,1)S(1)} async-done(((bf16[128,4,256]{2,0,1:T(8,128)(2,1)}), bf16[128,4,256]{2,0,1:T(8,128)(2,1)S(1)}, u32[]{:S(2)}, u32[]{:S(2)}) %all-to-all-start.2) | async-done | bytes 262176 | tf_op jit(solution)/shard_map/all_to_all | solution.py:81
  18.1 3.4 %all-to-all-start.3 = ((bf16[128,4,256]{2,0,1:T(8,128)(2,1)}), bf16[128,4,256]{2,0,1:T(8,128)(2,1)S(1)}, u32[]{:S(2)}, u32[]{:S(2)}) async-start(bf16[128,4,256]{2,0,1:T(8,128)(2,1)} %copy.28), calls=%async_computation.3 | async-start | bytes 524288 | tf_op jit(solution)/shard_map/all_to_all | solution.py:82
  21.5 3.3 all_to_all.72
  24.9 2.5 copy.25
  27.3 4.2 %all-to-all-start = ((bf16[128,4,2048]{2,0,1:T(8,128)(2,1)}), bf16[128,4,2048]{2,0,1:T(8,128)(2,1)S(1)}, u32[]{:S(2)}, u32[]{:S(2)}) async-start(bf16[128,4,2048]{2,0,1:T(8,128)(2,1)} %copy.25), calls=%async_computation | async-start | bytes 4194304 | tf_op jit(solution)/shard_map/all_to_all | solution.py:80
  31.5 4.5 %all_to_all.75 = bf16[128,4,2048]{2,1,0:T(4,128)(2,1)} reshape(bf16[1,128,8192]{2,1,0:T(8,128)(2,1)} %param.13) | data formatting | bytes 4194304 | tf_op jit(solution)/shard_map/all_to_all | solution.py:83
  36.0 4.1 %copy.26 = bf16[128,4,2048]{2,0,1:T(8,128)(2,1)} copy(bf16[128,4,2048]{2,1,0:T(4,128)(2,1)} %all_to_all.75) | data formatting | bytes 4194304 | tf_op jit(solution)/shard_map/all_to_all | solution.py:83
  40.1 14.6 %all-to-all-done = bf16[128,4,2048]{2,0,1:T(8,128)(2,1)S(1)} async-done(((bf16[128,4,2048]{2,0,1:T(8,128)(2,1)}), bf16[128,4,2048]{2,0,1:T(8,128)(2,1)S(1)}, u32[]{:S(2)}, u32[]{:S(2)}) %all-to-all-start) | async-done | bytes 2097184 | tf_op jit(solution)/shard_map/all_to_all | solution.py:80
  54.7 4.4 %all-to-all-start.1 = ((bf16[128,4,2048]{2,0,1:T(8,128)(2,1)}), bf16[128,4,2048]{2,0,1:T(8,128)(2,1)}, u32[]{:S(2)}, u32[]{:S(2)}) async-start(bf16[128,4,2048]{2,0,1:T(8,128)(2,1)} %copy.26), calls=%async_computation.1 | async-start | bytes 4194304 | tf_op jit(solution)/shard_map/all_to_all | solution.py:83
  59.2 26.0 %all-gather = s32[1,512]{1,0:T(1,128)S(1)} all-gather(s32[1,128]{1,0:T(1,128)S(1)} %copy-done.8), channel_id=2, replica_groups=mesh['section'=8,'seq'=4] {'seq'}, dimensions={1}, use_global_device_ids=true | all-gather | bytes 2560 | tf_op jit(solution)/shard_map/all_gather | solution.py:85
  85.4 2.2 copy.47
  87.7 3.7 %copy.48 = bf16[64,8,16,128]{3,2,1,0:T(8,128)(2,1)} copy(bf16[64,8,16,128]{3,1,2,0:T(8,128)(2,1)} %bitcast.38) | data formatting | bytes 4194304
  91.4 33.2 %collective-permute-done = bf16[128,8192]{1,0:T(8,128)(2,1)} collective-permute-done((bf16[128,8192]{1,0:T(8,128)(2,1)}, bf16[128,8192]{1,0:T(8,128)(2,1)}, u32[]{:S(2)}, u32[]{:S(2)}) %collective-permute-start) | collective-permute-done | bytes 2097184 | tf_op jit(solution)/shard_map/ppermute | solution.py:78
  124.6 4.0 %pad_maximum_fusion = bf16[256,8192]{1,0:T(8,128)(2,1)} fusion(bf16[128,8192]{1,0:T(8,128)(2,1)} %collective-permute-done, bf16[128,8192]{1,0:T(8,128)(2,1)S(1)} %bitcast.127), kind=kLoop, calls=%fused_computation.43 | loop fusion | flops 8388608 | bytes 8388608 | tf_op jit(solution)/shard_map/concatenate | solution.py:93
  128.6 110.8 %while.32 = (s32[]{:T(128)}, bf16[2,8,512,128]{3,2,1,0:T(8,128)(2,1)}, bf16[2,512,128]{2,1,0:T(8,128)(2,1)}, bf16[2,512,128]{2,1,0:T(8,128)(2,1)}, bf16[2,8,512,...) while((s32[]{:T(128)}, ...), condition=%wide.region_6.7_spmd.clone, body=%wide.region_0.6_spmd.clone.sunk | while | flops 407894528 | bytes 49566240 | solution.py:60
  132.8 48.1 %while.33 = (s32[]{:T(128)}, f32[512,128]{1,0:T(8,128)S(1)}, f32[512,128]{1,0:T(8,128)S(1)}, bf16[8,512,128]{2,1,0:T(8,128)(2,1)}, bf16[8,512,128]{2,1,0:T(8,128...) while((s32[]{:T(128)}, f32[512,128]{1,0:T(8,128)S(1)}, ...), condition=%wide.region_5.5_spmd.clone, body=%wide.region_1.4_spmd.clone.sunk | while | flops 406977024 | bytes 10242200 | solution.py:39
  134.9 1.3 fusion.68
  180.9 2.4 bitcast_dynamic-update-slice_fusion.5
  188.2 48.1 %while.33 = (s32[]{:T(128)}, f32[512,128]{1,0:T(8,128)S(1)}, f32[512,128]{1,0:T(8,128)S(1)}, bf16[8,512,128]{2,1,0:T(8,128)(2,1)}, bf16[8,512,128]{2,1,0:T(8,128...) while((s32[]{:T(128)}, f32[512,128]{1,0:T(8,128)S(1)}, ...), condition=%wide.region_5.5_spmd.clone, body=%wide.region_1.4_spmd.clone.sunk | while | flops 406977024 | bytes 10242200 | solution.py:39
  196.4 1.3 fusion.68
  236.3 2.4 bitcast_dynamic-update-slice_fusion.5
  241.5 4.2 %all-to-all-start.5 = ((bf16[4,128,256]{2,1,0:T(8,128)(2,1)}), bf16[4,128,256]{2,1,0:T(8,128)(2,1)S(1)}, u32[]{:S(2)}, u32[]{:S(2)}) async-start(bf16[4,128,256]{2,1,0:T(8,128)(2,1)} %all_to_all.87), calls=%async_computation.5 | async-start | bytes 524288 | tf_op jit(solution)/shard_map/all_to_all | solution.py:91
  245.8 2.9 copy.33
  248.7 2.3 all_to_all.84
  251.0 3.8 %all-to-all-done.5 = bf16[4,128,256]{2,1,0:T(8,128)(2,1)S(1)} async-done(((bf16[4,128,256]{2,1,0:T(8,128)(2,1)}), bf16[4,128,256]{2,1,0:T(8,128)(2,1)S(1)}, u32[]{:S(2)}, u32[]{:S(2)}) %all-to-all-start.5) | async-done | bytes 262176 | tf_op jit(solution)/shard_map/all_to_all | solution.py:91
  254.8 3.8 %all-to-all-start.4 = ((bf16[4,128,2048]{2,1,0:T(8,128)(2,1)}), bf16[4,128,2048]{2,1,0:T(8,128)(2,1)S(1)}, u32[]{:S(2)}, u32[]{:S(2)}) async-start(bf16[4,128,2048]{2,1,0:T(8,128)(2,1)} %all_to_all.84), calls=%async_computation.4 | async-start | bytes 4194304 | tf_op jit(solution)/shard_map/all_to_all | solution.py:90
  260.9 6.7 %collective-permute-done.1 = bf16[512,256]{0,1:T(8,128)(2,1)S(1)} collective-permute-done((bf16[512,256]{0,1:T(8,128)(2,1)}, bf16[512,256]{0,1:T(8,128)(2,1)S(1)}, u32[]{:S(2)}, u32[]{:S(2)}) %collective-permute-start.1) | collective-permute-done | bytes 262176 | tf_op jit(solution)/shard_map/ppermute | solution.py:95
  267.9 38.7 %all-to-all-done.4 = bf16[4,128,2048]{2,1,0:T(8,128)(2,1)S(1)} async-done(((bf16[4,128,2048]{2,1,0:T(8,128)(2,1)}), bf16[4,128,2048]{2,1,0:T(8,128)(2,1)S(1)}, u32[]{:S(2)}, u32[]{:S(2)}) %all-to-all-start.4) | async-done | bytes 2097184 | tf_op jit(solution)/shard_map/all_to_all | solution.py:90
  306.5 2.5 copy.34
  309.0 4.1 %copy.41 = bf16[1,128,8192]{2,1,0:T(8,128)(2,1)} copy(bf16[1,128,8192]{1,2,0:T(8,128)(2,1)} %bitcast.124) | data formatting | bytes 4194304
  313.1 12.6 %fusion.24 = bf16[1,8192,256]{2,1,0:T(8,128)(2,1)} fusion(bf16[1024,8192]{1,0:T(8,128)(2,1)} %all-gather.3.cloned.1.call-done, bf16[1024,256]{1,0:T(8,128)(2,1)S(1)} %bitcast.136), kind=kOutput, calls=%fused_computation.42 | convolution fusion | flops 4297064448 | bytes 21495808 | tf_op jit(solution)/shard_map/dot_general | solution.py:70
  (220 shorter events, 111.1 us)
Async XLA Ops:
  9.0 9.1 %all-to-all-start.2 = ((bf16[128,4,256]{2,0,1:T(8,128)(2,1)}), bf16[128,4,256]{2,0,1:T(8,128)(2,1)S(1)}, u32[]{:S(2)}, u32[]{:S(2)}) async-start(bf16[128,4,256]{2,0,1:T(8,128)(2,1)} %copy.27), calls=%async_computation.2 | async-start | bytes 524288 | tf_op jit(solution)/shard_map/all_to_all | solution.py:81
  18.1 9.2 %all-to-all-start.3 = ((bf16[128,4,256]{2,0,1:T(8,128)(2,1)}), bf16[128,4,256]{2,0,1:T(8,128)(2,1)S(1)}, u32[]{:S(2)}, u32[]{:S(2)}) async-start(bf16[128,4,256]{2,0,1:T(8,128)(2,1)} %copy.28), calls=%async_computation.3 | async-start | bytes 524288 | tf_op jit(solution)/shard_map/all_to_all | solution.py:82
  27.3 27.3 %all-to-all-start = ((bf16[128,4,2048]{2,0,1:T(8,128)(2,1)}), bf16[128,4,2048]{2,0,1:T(8,128)(2,1)S(1)}, u32[]{:S(2)}, u32[]{:S(2)}) async-start(bf16[128,4,2048]{2,0,1:T(8,128)(2,1)} %copy.25), calls=%async_computation | async-start | bytes 4194304 | tf_op jit(solution)/shard_map/all_to_all | solution.py:80
  31.5 93.1 %collective-permute-start = (bf16[128,8192]{1,0:T(8,128)(2,1)}, bf16[128,8192]{1,0:T(8,128)(2,1)}, u32[]{:S(2)}, u32[]{:S(2)}) collective-permute-start(bf16[128,8192]{1,0:T(8,128)(2,1)} %bitcast.126), channel_id=1, source_target_pairs={{0,28},{4,24},{8,20},{12,16},{16,12},{20,8},{24,4},{28,0},{1,29},{... | collective-permute-start | bytes 6291464 | tf_op jit(solution)/shard_map/ppermute | solution.py:78
  40.1 19.1 %copy-start.8 = (s32[1,128]{1,0:T(1,128)S(1)}, s32[1,128]{1,0:T(1,128)}, u32[]{:S(2)}) copy-start(s32[1,128]{1,0:T(1,128)} %param.15) | copy-start | bytes 1540
  54.7 4.5 %copy-start.3 = (bf16[128,4,2048]{2,0,1:T(8,128)(2,1)}, bf16[128,4,2048]{2,0,1:T(8,128)(2,1)S(1)}, u32[]{:S(2)}) copy-start(bf16[128,4,2048]{2,0,1:T(8,128)(2,1)S(1)} %all-to-all-done) | copy-start | bytes 6291460
  54.7 33.0 %all-to-all-start.1 = ((bf16[128,4,2048]{2,0,1:T(8,128)(2,1)}), bf16[128,4,2048]{2,0,1:T(8,128)(2,1)}, u32[]{:S(2)}, u32[]{:S(2)}) async-start(bf16[128,4,2048]{2,0,1:T(8,128)(2,1)} %copy.26), calls=%async_computation.1 | async-start | bytes 4194304 | tf_op jit(solution)/shard_map/all_to_all | solution.py:83
  59.1 253.9 %all-gather.3.cloned.1.call-start = ((), (), s32[]{:S(2)}) async-start(), calls=%async_computation.6 | async-start | bytes 20971520 | tf_op jit(solution)/shard_map/all_gather | solution.py:94
  87.7 36.9 %copy-start.6 = (bf16[1,128,8192]{2,1,0:T(8,128)(2,1)S(1)}, bf16[1,128,8192]{2,1,0:T(8,128)(2,1)}, u32[]{:S(2)}) copy-start(bf16[1,128,8192]{2,1,0:T(8,128)(2,1)} %param.14) | copy-start | bytes 6291460
  128.6 1.3 copy-start
  128.7 4.1 %copy-start.4 = (bf16[2,512,128]{2,1,0:T(8,128)(2,1)}, bf16[2,512,128]{2,1,0:T(8,128)(2,1)S(1)}, u32[]{:S(2)}) copy-start(bf16[2,512,128]{2,1,0:T(8,128)(2,1)S(1)} %get-tuple-element.437) | copy-start | bytes 786436 | tf_op jit(solution)/shard_map/while
  129.9 1.6 copy-start.2
  180.9 3.2 copy-start.1
  180.9 3.2 copy-start.5
  184.1 1.3 copy-start
  184.1 4.1 %copy-start.4 = (bf16[2,512,128]{2,1,0:T(8,128)(2,1)}, bf16[2,512,128]{2,1,0:T(8,128)(2,1)S(1)}, u32[]{:S(2)}) copy-start(bf16[2,512,128]{2,1,0:T(8,128)(2,1)S(1)} %get-tuple-element.437) | copy-start | bytes 786436 | tf_op jit(solution)/shard_map/while
  185.4 1.6 copy-start.2
  236.3 3.2 copy-start.1
  236.3 3.2 copy-start.5
  241.5 13.3 %all-to-all-start.5 = ((bf16[4,128,256]{2,1,0:T(8,128)(2,1)}), bf16[4,128,256]{2,1,0:T(8,128)(2,1)S(1)}, u32[]{:S(2)}, u32[]{:S(2)}) async-start(bf16[4,128,256]{2,1,0:T(8,128)(2,1)} %all_to_all.87), calls=%async_computation.5 | async-start | bytes 524288 | tf_op jit(solution)/shard_map/all_to_all | solution.py:91
  251.0 7.6 %copy-start.7 = (bf16[2,512,128]{2,1,0:T(8,128)(2,1)S(1)}, bf16[2,512,128]{2,1,0:T(8,128)(2,1)}, u32[]{:S(2)}) copy-start(bf16[2,512,128]{2,1,0:T(8,128)(2,1)} %get-tuple-element.103) | copy-start | bytes 786436
  254.8 51.7 %all-to-all-start.4 = ((bf16[4,128,2048]{2,1,0:T(8,128)(2,1)}), bf16[4,128,2048]{2,1,0:T(8,128)(2,1)S(1)}, u32[]{:S(2)}, u32[]{:S(2)}) async-start(bf16[4,128,2048]{2,1,0:T(8,128)(2,1)} %all_to_all.84), calls=%async_computation.4 | async-start | bytes 4194304 | tf_op jit(solution)/shard_map/all_to_all | solution.py:90
  259.4 8.2 %collective-permute-start.1 = (bf16[512,256]{0,1:T(8,128)(2,1)}, bf16[512,256]{0,1:T(8,128)(2,1)S(1)}, u32[]{:S(2)}, u32[]{:S(2)}) collective-permute-start(bf16[512,256]{0,1:T(8,128)(2,1)} %bitcast.18), channel_id=1, source_target_pairs={{0,28},{4,24},{8,20},{12,16},{16,12},{20,8},{24,4},{28,0},{1,29},{... | collective-permute-start | bytes 786440 | tf_op jit(solution)/shard_map/ppermute | solution.py:95
Sparse Core Ops, SparseCore 0:
  128.7 182.3 all-gather.2
where the time goes:
time: 335 us; the launch traced here: 333 us
  waiting for transfers between devices  100 us (30%)
  matrix products  85 us (25%)
  local copies, waits for them, and re-layouts  53.2 us (16%)
  other arithmetic  29 us (9%)
  blocking collectives  26 us (8%)
  starting transfers between devices  23.8 us (7%)
  between operations  14.2 us (4%)
    all_to_all x1, waiting for transfers between devices, local(): lax.all_to_all(query_out, 'seq', split_axis=0, concat_axis=1, tiled=True)  38.7 us
    ppermute x1, waiting for transfers between devices, local(): mirror_rows = lax.ppermute(layer_input[0], 'section', mirror)  33.2 us
    all_gather x1, blocking collectives, local(): doc_ids = lax.all_gather(doc_segments[0], 'seq', axis=0, tiled=True)  26 us
    dot_general x16, matrix products, one_head(): dprobs = jnp.dot(grad_one, value_col.T, preferred_element_type=jnp.float32)  20.4 us
    dot_general x16, matrix products, one_head(): jnp.dot(probs_low.T, grad_one, preferred_element_type=jnp.float32)  19.7 us
    reduce_sum x16, other arithmetic, one_head(): jnp.sum(grad_one.astype(jnp.float32) * attended.astype(jnp.float32), axis...  17.2 us
    dot_general x16, matrix products, one_head(): jnp.dot(dscores, key_col, preferred_element_type=jnp.float32)  16.1 us
    all_to_all x1, waiting for transfers between devices, local(): lax.all_to_all(queries[0], 'seq', split_axis=1, concat_axis=0, tiled=True)  14.6 us
  transfers between devices with their start and end apart: 9, of which 6 were waited for; matrix products, arithmetic and copies ran while one was open for 40% of the time, Pallas kernels for 0%

commit v1 on v0

--- a/solution.py
+++ b/solution.py
@@ -5,6 +5,27 @@
 from jax.sharding import PartitionSpec as P
 
 HEAD_WIDTH = 128
+
+
+def _meet_blocks(a0):
+    chip_axis = "seq"
+    block_now, v1 = (jax.lax.axis_size(chip_axis), jax.lax.axis_index(chip_axis))
+    near = list(a0.shape)
+    current_arr = a0.shape[1] // block_now
+    near[1] = current_arr
+    y = near[0]
+    near[0] = y * block_now
+    current_block = jnp.zeros(near, a0.dtype)
+    idx = 0
+    while idx < block_now:
+        n_now = lax.dynamic_slice_in_dim(a0, (v1 ^ idx) * current_arr, current_arr, axis=1)
+        if idx:
+            n_now = jax.lax.ppermute(n_now, chip_axis, [(k, k ^ idx) for k in range(block_now)])
+        current_block = lax.dynamic_update_slice_in_dim(
+            current_block, n_now, (v1 ^ idx) * y, axis=0
+        )
+        idx += 1
+    return current_block
 
 
 def group_pass(query_group, key_col, value_col, grad_group, allowed):
@@ -77,7 +98,7 @@
     mirror = [(i, section_count - 1 - i) for i in range(section_count)]
     mirror_rows = lax.ppermute(layer_input[0], "section", mirror)
     query_head, key_head, value_head, grad_head = (
-        lax.all_to_all(queries[0], "seq", split_axis=1, concat_axis=0, tiled=True),
+        _meet_blocks(queries[0]),
         lax.all_to_all(key_states[0], "seq", split_axis=1, concat_axis=0, tiled=True),
         lax.all_to_all(section_value_states[0], "seq", split_axis=1, concat_axis=0, tiled=True),
         lax.all_to_all(out_grad[0], "seq", split_axis=1, concat_axis=0, tiled=True),

time: 335 us -> 312 us (0.931)
  waiting for transfers between devices: 100 us -> 64.3 us
  blocking collectives: 26 us -> 33.7 us
  local copies, waits for them, and re-layouts: 53.2 us -> 59.6 us
    ppermute x1, waiting for transfers between devices: 33.2 us -> 11.5 us  [local(): mirror_rows = lax.ppermute(layer_input[0], 'section', mirror)]
    all_to_all x1 -> x0, waiting for transfers between devices: 14.6 us -> none  [local(): lax.all_to_all(queries[0], 'seq', split_axis=1, concat_axis=0, tiled=True)]
    dynamic_slice x0 -> x5, local copies, waits for them, and re-layouts: none -> 8.02 us  [_meet_blocks(): lax.dynamic_slice_in_dim(a0, (v1 ^ idx) * current_arr, current_arr, axis=1)]
    all_gather x1, blocking collectives: 26 us -> 33.7 us  [local(): doc_ids = lax.all_gather(doc_segments[0], 'seq', axis=0, tiled=True)]
    dynamic_update_slice x0 -> x4, local copies, waits for them, and re-layouts: none -> 6.68 us  [_meet_blocks(): lax.dynamic_update_slice_in_dim(current_block, n_now, (v1 ^ idx) * y, axi...]
    dynamic_slice x8, local copies, waits for them, and re-layouts: 2.85 us -> 9.09 us  [attention_grads(): lax.map(per_group, (query_split, key_split, value_split, grad_split))]
    all_to_all x2 -> x0, local copies, waits for them, and re-layouts: 5.79 us -> none  [local(): lax.all_to_all(queries[0], 'seq', split_axis=1, concat_axis=0, tiled=True)]
    all_to_all x1 -> x0, starting transfers between devices: 4.15 us -> none  [local(): lax.all_to_all(queries[0], 'seq', split_axis=1, concat_axis=0, tiled=True)]
  transfers between devices with their start and end apart: 9 -> 11, of which waited for: 6 -> 5; matrix products, arithmetic and copies ran while one was open for 40% -> 47% of each run, Pallas kernels for 0% -> 0%
where the time goes in v1:
time: 312 us; the launch traced here: 309 us
  matrix products  85 us (27%)
  waiting for transfers between devices  64.3 us (21%)
  local copies, waits for them, and re-layouts  59.6 us (19%)
  blocking collectives  33.7 us (11%)
  other arithmetic  27.7 us (9%)
  starting transfers between devices  23.9 us (8%)
  between operations  14.2 us (5%)
    all_to_all x1, waiting for transfers between devices, local(): lax.all_to_all(query_out, 'seq', split_axis=0, concat_axis=1, tiled=True)  38.3 us
    all_gather x1, blocking collectives, local(): doc_ids = lax.all_gather(doc_segments[0], 'seq', axis=0, tiled=True)  33.7 us
    dot_general x16, matrix products, one_head(): dprobs = jnp.dot(grad_one, value_col.T, preferred_element_type=jnp.float32)  20.4 us
    dot_general x16, matrix products, one_head(): jnp.dot(probs_low.T, grad_one, preferred_element_type=jnp.float32)  19.7 us
    reduce_sum x16, other arithmetic, one_head(): jnp.sum(grad_one.astype(jnp.float32) * attended.astype(jnp.float32), axis...  17.2 us
    dot_general x16, matrix products, one_head(): jnp.dot(dscores, key_col, preferred_element_type=jnp.float32)  16.1 us
    dot_general x1, matrix products, row_product(): lax.dot_general(shard_rows, value_rows, (((0,), (0,)), ((), ())), preferr...  12.6 us
    ppermute x1, waiting for transfers between devices, local(): mirror_rows = lax.ppermute(layer_input[0], 'section', mirror)  11.5 us
  transfers between devices with their start and end apart: 11, of which 5 were waited for; matrix products, arithmetic and copies ran while one was open for 47% of the time, Pallas kernels for 0%

profile of v1, /device:TPU:8, one launch (start us, length us, event | category | flops | bytes accessed | tf_op | source)
XLA Modules:
  0.0 309.3 jit_solution(12901176355108206026)
XLA Ops:
  10.1 3.7 %all-to-all-start.1 = ((bf16[128,4,256]{2,0,1:T(8,128)(2,1)}), bf16[128,4,256]{2,0,1:T(8,128)(2,1)S(1)}, u32[]{:S(2)}, u32[]{:S(2)}) async-start(bf16[128,4,256]{2,0,1:T(8,128)(2,1)} %copy.33), calls=%async_computation.1 | async-start | bytes 524288 | tf_op jit(solution)/shard_map/all_to_all | solution.py:102
  15.7 4.2 %all-to-all-done.1 = bf16[128,4,256]{2,0,1:T(8,128)(2,1)S(1)} async-done(((bf16[128,4,256]{2,0,1:T(8,128)(2,1)}), bf16[128,4,256]{2,0,1:T(8,128)(2,1)S(1)}, u32[]{:S(2)}, u32[]{:S(2)}) %all-to-all-start.1) | async-done | bytes 262176 | tf_op jit(solution)/shard_map/all_to_all | solution.py:102
  19.9 3.4 %all-to-all-start.2 = ((bf16[128,4,256]{2,0,1:T(8,128)(2,1)}), bf16[128,4,256]{2,0,1:T(8,128)(2,1)S(1)}, u32[]{:S(2)}, u32[]{:S(2)}) async-start(bf16[128,4,256]{2,0,1:T(8,128)(2,1)} %copy.34), calls=%async_computation.2 | async-start | bytes 524288 | tf_op jit(solution)/shard_map/all_to_all | solution.py:103
  23.3 3.3 %all_to_all.60 = bf16[128,4,2048]{2,1,0:T(4,128)(2,1)S(1)} reshape(bf16[1,128,8192]{2,1,0:T(8,128)(2,1)} %param.13) | data formatting | bytes 4194304 | tf_op jit(solution)/shard_map/all_to_all | solution.py:104
  26.6 2.5 copy.32
  29.1 4.2 %all-to-all-start = ((bf16[128,4,2048]{2,0,1:T(8,128)(2,1)}), bf16[128,4,2048]{2,0,1:T(8,128)(2,1)S(1)}, u32[]{:S(2)}, u32[]{:S(2)}) async-start(bf16[128,4,2048]{2,0,1:T(8,128)(2,1)} %copy.32), calls=%async_computation | async-start | bytes 4194304 | tf_op jit(solution)/shard_map/all_to_all | solution.py:104
  33.3 2.7 constant_dynamic-slice_fusion.2
  36.0 2.0 copy.29
  38.0 2.0 collective-permute-start
  40.0 2.0 copy.30
  47.1 33.7 %all-gather = s32[1,512]{1,0:T(1,128)S(1)} all-gather(s32[1,128]{1,0:T(1,128)S(1)} %copy-done.10), channel_id=2, replica_groups=mesh['section'=8,'seq'=4] {'seq'}, dimensions={1}, use_global_device_ids=true | all-gather | bytes 2560 | tf_op jit(solution)/shard_map/all_gather | solution.py:106
  81.0 2.0 constant_dynamic-update-slice_fusion.2
  83.0 2.0 constant_dynamic-update-slice_fusion.1
  84.9 1.9 constant_dynamic-update-slice_fusion
  86.9 2.0 copy.53
  88.8 11.5 %collective-permute-done.3 = bf16[128,8192]{1,0:T(8,128)(2,1)} collective-permute-done((bf16[128,8192]{1,0:T(8,128)(2,1)}, bf16[128,8192]{1,0:T(8,128)(2,1)}, u32[]{:S(2)}, u32[]{:S(2)}) %collective-permute-start.3) | collective-permute-done | bytes 2097184 | tf_op jit(solution)/shard_map/ppermute | solution.py:99
  100.3 4.0 %pad_maximum_fusion = bf16[256,8192]{1,0:T(8,128)(2,1)} fusion(bf16[128,8192]{1,0:T(8,128)(2,1)} %collective-permute-done.3, bf16[128,8192]{1,0:T(8,128)(2,1)S(1)} %bitcast.125), kind=kLoop, calls=%fused_computation.42 | loop fusion | flops 8388608 | bytes 8388608 | tf_op jit(solution)/shard_map/concatenate | solution.py:114
  104.3 112.3 %while.32 = (s32[]{:T(128)}, bf16[2,8,512,128]{3,2,1,0:T(8,128)(2,1)}, bf16[2,512,128]{2,1,0:T(8,128)(2,1)}, bf16[2,512,128]{2,1,0:T(8,128)(2,1)}, bf16[2,8,512,...) while((s32[]{:T(128)}, ...), condition=%wide.region_6.7_spmd.clone, body=%wide.region_0.6_spmd.clone.sunk | while | flops 407894528 | bytes 28594748 | solution.py:81
  109.2 48.1 %while.33 = (s32[]{:T(128)}, f32[512,128]{1,0:T(8,128)S(1)}, f32[512,128]{1,0:T(8,128)S(1)}, bf16[8,512,128]{2,1,0:T(8,128)(2,1)}, bf16[8,512,128]{2,1,0:T(8,128...) while((s32[]{:T(128)}, f32[512,128]{1,0:T(8,128)S(1)}, ...), condition=%wide.region_5.5_spmd.clone, body=%wide.region_1.4_spmd.clone.sunk | while | flops 406977024 | bytes 10242200 | solution.py:60
  157.4 2.3 bitcast_dynamic-update-slice_fusion.6
  165.4 48.0 %while.33 = (s32[]{:T(128)}, f32[512,128]{1,0:T(8,128)S(1)}, f32[512,128]{1,0:T(8,128)S(1)}, bf16[8,512,128]{2,1,0:T(8,128)(2,1)}, bf16[8,512,128]{2,1,0:T(8,128...) while((s32[]{:T(128)}, f32[512,128]{1,0:T(8,128)S(1)}, ...), condition=%wide.region_5.5_spmd.clone, body=%wide.region_1.4_spmd.clone.sunk | while | flops 406977024 | bytes 10242200 | solution.py:60
  213.5 2.3 bitcast_dynamic-update-slice_fusion.6
  218.8 3.7 %all-to-all-start.4 = ((bf16[4,128,256]{2,1,0:T(8,128)(2,1)}), bf16[4,128,256]{2,1,0:T(8,128)(2,1)S(1)}, u32[]{:S(2)}, u32[]{:S(2)}) async-start(bf16[4,128,256]{2,1,0:T(8,128)(2,1)} %all_to_all.72), calls=%async_computation.4 | async-start | bytes 524288 | tf_op jit(solution)/shard_map/all_to_all | solution.py:112
  222.5 2.9 copy.39
  225.4 2.3 all_to_all.69
  227.7 3.8 %all-to-all-done.4 = bf16[4,128,256]{2,1,0:T(8,128)(2,1)S(1)} async-done(((bf16[4,128,256]{2,1,0:T(8,128)(2,1)}), bf16[4,128,256]{2,1,0:T(8,128)(2,1)S(1)}, u32[]{:S(2)}, u32[]{:S(2)}) %all-to-all-start.4) | async-done | bytes 262176 | tf_op jit(solution)/shard_map/all_to_all | solution.py:112
  231.6 3.8 %all-to-all-start.3 = ((bf16[4,128,2048]{2,1,0:T(8,128)(2,1)}), bf16[4,128,2048]{2,1,0:T(8,128)(2,1)S(1)}, u32[]{:S(2)}, u32[]{:S(2)}) async-start(bf16[4,128,2048]{2,1,0:T(8,128)(2,1)} %all_to_all.69), calls=%async_computation.3 | async-start | bytes 4194304 | tf_op jit(solution)/shard_map/all_to_all | solution.py:111
  238.3 6.5 %collective-permute-done.4 = bf16[512,256]{0,1:T(8,128)(2,1)S(1)} collective-permute-done((bf16[512,256]{0,1:T(8,128)(2,1)}, bf16[512,256]{0,1:T(8,128)(2,1)S(1)}, u32[]{:S(2)}, u32[]{:S(2)}) %collective-permute-start.4) | collective-permute-done | bytes 262176 | tf_op jit(solution)/shard_map/ppermute | solution.py:116
  245.0 38.3 %all-to-all-done.3 = bf16[4,128,2048]{2,1,0:T(8,128)(2,1)S(1)} async-done(((bf16[4,128,2048]{2,1,0:T(8,128)(2,1)}), bf16[4,128,2048]{2,1,0:T(8,128)(2,1)S(1)}, u32[]{:S(2)}, u32[]{:S(2)}) %all-to-all-start.3) | async-done | bytes 2097184 | tf_op jit(solution)/shard_map/all_to_all | solution.py:111
  283.3 2.5 copy.40
  285.8 4.1 %copy.47 = bf16[1,128,8192]{2,1,0:T(8,128)(2,1)} copy(bf16[1,128,8192]{1,2,0:T(8,128)(2,1)} %bitcast.122) | data formatting | bytes 4194304
  289.9 12.6 %fusion.24 = bf16[1,8192,256]{2,1,0:T(8,128)(2,1)} fusion(bf16[1024,8192]{1,0:T(8,128)(2,1)} %all-gather.3.cloned.1.call-done, bf16[1024,256]{1,0:T(8,128)(2,1)S(1)} %bitcast.137), kind=kOutput, calls=%fused_computation.41 | convolution fusion | flops 4297064448 | bytes 21495808 | tf_op jit(solution)/shard_map/dot_general | solution.py:91
  (237 shorter events, 122.0 us)
Async XLA Ops:
  7.2 93.1 %collective-permute-start.3 = (bf16[128,8192]{1,0:T(8,128)(2,1)}, bf16[128,8192]{1,0:T(8,128)(2,1)}, u32[]{:S(2)}, u32[]{:S(2)}) collective-permute-start(bf16[128,8192]{1,0:T(8,128)(2,1)} %bitcast.124), channel_id=1, source_target_pairs={{0,28},{4,24},{8,20},{12,16},{16,12},{20,8},{24,4},{28,0},{1,29},{... | collective-permute-start | bytes 6291464 | tf_op jit(solution)/shard_map/ppermute | solution.py:99
  10.1 9.8 %all-to-all-start.1 = ((bf16[128,4,256]{2,0,1:T(8,128)(2,1)}), bf16[128,4,256]{2,0,1:T(8,128)(2,1)S(1)}, u32[]{:S(2)}, u32[]{:S(2)}) async-start(bf16[128,4,256]{2,0,1:T(8,128)(2,1)} %copy.33), calls=%async_computation.1 | async-start | bytes 524288 | tf_op jit(solution)/shard_map/all_to_all | solution.py:102
  19.9 9.2 %all-to-all-start.2 = ((bf16[128,4,256]{2,0,1:T(8,128)(2,1)}), bf16[128,4,256]{2,0,1:T(8,128)(2,1)S(1)}, u32[]{:S(2)}, u32[]{:S(2)}) async-start(bf16[128,4,256]{2,0,1:T(8,128)(2,1)} %copy.34), calls=%async_computation.2 | async-start | bytes 524288 | tf_op jit(solution)/shard_map/all_to_all | solution.py:103
  29.1 4.2 %copy-start.3 = (bf16[128,4,256]{2,0,1:T(8,128)(2,1)}, bf16[128,4,256]{2,0,1:T(8,128)(2,1)S(1)}, u32[]{:S(2)}) copy-start(bf16[128,4,256]{2,0,1:T(8,128)(2,1)S(1)} %all-to-all-done.2) | copy-start | bytes 786436
  29.1 57.7 %all-to-all-start = ((bf16[128,4,2048]{2,0,1:T(8,128)(2,1)}), bf16[128,4,2048]{2,0,1:T(8,128)(2,1)S(1)}, u32[]{:S(2)}, u32[]{:S(2)}) async-start(bf16[128,4,2048]{2,0,1:T(8,128)(2,1)} %copy.32), calls=%async_computation | async-start | bytes 4194304 | tf_op jit(solution)/shard_map/all_to_all | solution.py:104
  33.3 256.6 %all-gather.3.cloned.1.call-start = ((), (), s32[]{:S(2)}) async-start(), calls=%async_computation.5 | async-start | bytes 20971520 | tf_op jit(solution)/shard_map/all_gather | solution.py:115
  38.0 43.0 %collective-permute-start = (bf16[128,2048]{0,1:T(8,128)(2,1)}, bf16[128,2048]{0,1:T(8,128)(2,1)}, u32[]{:S(2)}, u32[]{:S(2)}) collective-permute-start(bf16[128,2048]{0,1:T(8,128)(2,1)} %bitcast.136), channel_id=1, source_target_pairs={{0,1},{1,0},{2,3},{3,2},{4,5},{5,4},{6,7},{7,6},{8,9},{9,8},{10,11... | collective-permute-start | bytes 1572872 | tf_op jit(solution)/shard_map/ppermute | solution.py:23
  42.1 40.9 %collective-permute-start.1 = (bf16[128,2048]{0,1:T(8,128)(2,1)}, bf16[128,2048]{0,1:T(8,128)(2,1)}, u32[]{:S(2)}, u32[]{:S(2)}) collective-permute-start(bf16[128,2048]{0,1:T(8,128)(2,1)} %bitcast.135), channel_id=1, source_target_pairs={{0,2},{1,3},{2,0},{3,1},{4,6},{5,7},{6,4},{7,5},{8,10},{9,11},{10,... | collective-permute-start | bytes 1572872 | tf_op jit(solution)/shard_map/ppermute | solution.py:23
  44.5 40.4 %collective-permute-start.2 = (bf16[128,2048]{0,1:T(8,128)(2,1)}, bf16[128,2048]{0,1:T(8,128)(2,1)}, u32[]{:S(2)}, u32[]{:S(2)}) collective-permute-start(bf16[128,2048]{0,1:T(8,128)(2,1)} %bitcast.134), channel_id=1, source_target_pairs={{0,3},{1,2},{2,1},{3,0},{4,7},{5,6},{6,5},{7,4},{8,11},{9,10},{10,... | collective-permute-start | bytes 1572872 | tf_op jit(solution)/shard_map/ppermute | solution.py:23
  44.5 2.6 copy-start.10
  44.8 36.1 %copy-start.4 = (bf16[128,4,256]{2,0,1:T(8,128)(2,1)S(1)}, bf16[128,4,256]{2,0,1:T(8,128)(2,1)}, u32[]{:S(2)}) copy-start(bf16[128,4,256]{2,0,1:T(8,128)(2,1)} %copy-done.3) | copy-start | bytes 786436
  86.9 13.4 %copy-start.2 = (bf16[1,128,8192]{2,1,0:T(8,128)(2,1)S(1)}, bf16[1,128,8192]{2,1,0:T(8,128)(2,1)}, u32[]{:S(2)}) copy-start(bf16[1,128,8192]{2,1,0:T(8,128)(2,1)} %param.14) | copy-start | bytes 6291460
  104.4 4.8 %copy-start = (bf16[2,512,128]{2,1,0:T(8,128)(2,1)}, bf16[2,512,128]{2,1,0:T(8,128)(2,1)S(1)}, u32[]{:S(2)}) copy-start(bf16[2,512,128]{2,1,0:T(8,128)(2,1)S(1)} %get-tuple-element.441) | copy-start | bytes 786436 | tf_op jit(solution)/shard_map/while
  157.4 2.4 copy-start.5
  157.4 2.4 copy-start.8
  157.4 3.2 %copy-start.1 = (bf16[2,512,128]{2,1,0:T(8,128)(2,1)S(1)}, bf16[2,512,128]{2,1,0:T(8,128)(2,1)}, u32[]{:S(2)}) copy-start(bf16[2,512,128]{2,1,0:T(8,128)(2,1)} %copy-done) | copy-start | bytes 786436 | tf_op jit(solution)/shard_map/while
  159.8 0.7 copy-start.6
  159.8 0.8 copy-start.9
  160.6 4.8 %copy-start = (bf16[2,512,128]{2,1,0:T(8,128)(2,1)}, bf16[2,512,128]{2,1,0:T(8,128)(2,1)S(1)}, u32[]{:S(2)}) copy-start(bf16[2,512,128]{2,1,0:T(8,128)(2,1)S(1)} %get-tuple-element.441) | copy-start | bytes 786436 | tf_op jit(solution)/shard_map/while
  213.5 2.4 copy-start.5
  213.5 2.4 copy-start.8
  213.5 3.2 %copy-start.1 = (bf16[2,512,128]{2,1,0:T(8,128)(2,1)S(1)}, bf16[2,512,128]{2,1,0:T(8,128)(2,1)}, u32[]{:S(2)}) copy-start(bf16[2,512,128]{2,1,0:T(8,128)(2,1)} %copy-done) | copy-start | bytes 786436 | tf_op jit(solution)/shard_map/while
  215.9 0.7 copy-start.6
  215.9 0.8 copy-start.9
  218.8 12.8 %all-to-all-start.4 = ((bf16[4,128,256]{2,1,0:T(8,128)(2,1)}), bf16[4,128,256]{2,1,0:T(8,128)(2,1)S(1)}, u32[]{:S(2)}, u32[]{:S(2)}) async-start(bf16[4,128,256]{2,1,0:T(8,128)(2,1)} %all_to_all.72), calls=%async_computation.4 | async-start | bytes 524288 | tf_op jit(solution)/shard_map/all_to_all | solution.py:112
  227.7 7.6 %copy-start.7 = (bf16[2,512,128]{2,1,0:T(8,128)(2,1)S(1)}, bf16[2,512,128]{2,1,0:T(8,128)(2,1)}, u32[]{:S(2)}) copy-start(bf16[2,512,128]{2,1,0:T(8,128)(2,1)} %get-tuple-element.103) | copy-start | bytes 786436
  231.6 51.8 %all-to-all-start.3 = ((bf16[4,128,2048]{2,1,0:T(8,128)(2,1)}), bf16[4,128,2048]{2,1,0:T(8,128)(2,1)S(1)}, u32[]{:S(2)}, u32[]{:S(2)}) async-start(bf16[4,128,2048]{2,1,0:T(8,128)(2,1)} %all_to_all.69), calls=%async_computation.3 | async-start | bytes 4194304 | tf_op jit(solution)/shard_map/all_to_all | solution.py:111
  236.2 8.6 %collective-permute-start.4 = (bf16[512,256]{0,1:T(8,128)(2,1)}, bf16[512,256]{0,1:T(8,128)(2,1)S(1)}, u32[]{:S(2)}, u32[]{:S(2)}) collective-permute-start(bf16[512,256]{0,1:T(8,128)(2,1)} %bitcast.22), channel_id=1, source_target_pairs={{0,28},{4,24},{8,20},{12,16},{16,12},{20,8},{24,4},{28,0},{1,29},{... | collective-permute-start | bytes 786440 | tf_op jit(solution)/shard_map/ppermute | solution.py:116
Sparse Core Ops, SparseCore 0:
  104.5 182.8 all-gather.2
